TPU v7x, 32 devices: a whole 2x2x4 slice. The times are simulated.
32 devices in a mesh: row: 4 (over y, core), col: 8 (over z, x).
Axes of the slice: x: 2, y: 2, z: 4, core: 2. Of those that a mesh axis runs over, the one named last changes fastest.
Arguments:
- tokens: bfloat16 [512, 16384], P('col', 'row'), may hold values from -6 to 6
- gate_packed: bfloat16 [2560, 1024, 128], P('row', 'col'), may hold values from -0.0625 to 0.0625
- up_packed: bfloat16 [2560, 1024, 128], P('row', 'col'), may hold values from -0.0625 to 0.0625
- down_packed: bfloat16 [5120, 512, 128], P('col', 'row'), may hold values from -0.0546875 to 0.0546875
- gate_keep: int32 [128, 208], P('row', 'col'), may hold values from 0 to 1, as said below
- down_keep: int32 [208, 128], P('col', 'row'), may hold values from 0 to 1, as said below
Outputs:
- mixed: bfloat16 [512, 16384], P('col', 'row')
Inputs may be any that keep to these rules, and one draw needn't show every extreme that they name: `gate_keep`: in every tile of 32 x 26 blocks, at least 160 and at most 640 blocks are kept; some tile keeps exactly 640. `down_keep`: in every tile of 26 x 32 blocks, at least 160 and at most 640 blocks are kept; some tile keeps exactly 640.
All inputs are finite; a program needn't handle non-finite values.
Results may differ from a plain program's by a relative error of at most 0.02.
Values may be sent and summed in bfloat16 or wider, within the bound.
No kernel may reach another device: no remote copies, remote signals or barrier semaphores. Data moves between devices by JAX's collectives and lax.ppermute only.
A program may use at most 320 MiB of HBM per device.

v0:
```python
import jax
import jax.numpy as jnp
from jax import lax
from jax.sharding import PartitionSpec as P


def dense_tile(packed_tile, keep_tile):
    in_blocks, out_blocks = keep_tile.shape
    block = packed_tile.shape[2]
    flattened = keep_tile.reshape(-1)
    position = jnp.cumsum(flattened) - 1
    slot_index = jnp.where(flattened == 1, position, 0)
    picked = (
        jnp.take(packed_tile, slot_index, axis=0)
        * flattened.astype(packed_tile.dtype)[:, None, None]
    )
    picked = picked.reshape(in_blocks, out_blocks, block, block).transpose(0, 2, 1, 3)
    return picked.reshape(in_blocks * block, out_blocks * block)


def local(tokens, gate_packed, up_packed, down_packed, gate_keep, down_keep):
    gate_dense = dense_tile(gate_packed, gate_keep)
    up_dense = dense_tile(up_packed, gate_keep)
    down_dense = dense_tile(down_packed, down_keep)
    segment = lax.all_gather(tokens, "col", axis=0, tiled=True)
    gate_rows = jnp.dot(segment, gate_dense, preferred_element_type=jnp.float32)
    up_rows = jnp.dot(segment, up_dense, preferred_element_type=jnp.float32)
    gate_sum, up_sum = (
        lax.psum(gate_rows.astype(jnp.bfloat16), "row").astype(jnp.float32),
        lax.psum(up_rows.astype(jnp.bfloat16), "row").astype(jnp.float32),
    )
    every_hidden = (jax.nn.silu(gate_sum) * up_sum).astype(jnp.bfloat16)
    partial_out = jnp.dot(every_hidden, down_dense, preferred_element_type=jnp.float32)
    summed = lax.psum_scatter(
        partial_out.astype(jnp.bfloat16), "col", scatter_dimension=0, tiled=True
    )
    return summed


def solution(mesh):
    in_specs = (
        P("col", "row"),
        P("row", "col", None),
        P("row", "col", None),
        P("col", "row", None),
        P("row", "col"),
        P("col", "row"),
    )
    out_specs = P("col", "row")
    return jax.shard_map(local, mesh=mesh, in_specs=in_specs, out_specs=out_specs, check_vma=False)
```

profile of v0, /device:TPU:0, one launch (start us, length us, event | category | flops | bytes accessed | tf_op | source)
XLA Modules:
  0.0 474.2 jit_solution(3464177804756279992)
XLA Ops:
  6.5 0.7 all-gather.2.cloned.1.call-update
  7.3 0.8 reshape.68
  8.1 0.3 reduce-window.16
  8.4 0.1 slice.20
  8.5 0.1 slice_reduce_fusion.1
  8.6 0.1 add_bitcast_fusion.1
  8.7 27.1 %gather_fusion = bf16[832,128,128]{2,1,0:T(8,128)(2,1)} fusion(bf16[640,128,128]{2,1,0:T(8,128)(2,1)} %param.9, s32[1024]{0:T(1024)S(1)} %pad_clamp_fusion.1), kind=kCustom, calls=%fused_computation.clone | custom fusion | bytes 54529280 | tf_op jit(solution)/shard_map/jit(_take)/gather | solution.py:14
  35.8 27.1 %gather_fusion.1 = bf16[832,128,128]{2,1,0:T(8,128)(2,1)} fusion(bf16[640,128,128]{2,1,0:T(8,128)(2,1)} %param.10, s32[1024]{0:T(1024)S(1)} %pad_clamp_fusion.1), kind=kCustom, calls=%fused_computation.1.clone | custom fusion | bytes 54529280 | tf_op jit(solution)/shard_map/jit(_take)/gather | solution.py:14
  63.0 36.9 %select_multiply_fusion.2 = (bf16[832,128,128]{2,1,0:T(8,128)(2,1)}, bf16[832,128,128]{2,1,0:T(8,128)(2,1)}) fusion(bf16[832,128,128]{2,1,0:T(8,128)(2,1)} %gather_fusion, pred[832]{0:T(1024)(128)(4,1)S(1)} %get-tuple-element.8, bf16[832]{0:T(1024)(128)(2,1)S(1)} %convert_element_type.39, bf16[832,128,128]{2,1,0:T(8,128)(2,1)} %gather_fusion.1), kind=kLoop, calls=%fused_computation.14 | loop fusion | flops 54525952 | bytes 109054400 | tf_op jit(solution)/shard_map/mul | solution.py:14
  99.9 35.0 %copy.8 = bf16[32,26,128,128]{2,0,3,1:T(8,128)(2,1)} copy(bf16[32,26,128,128]{3,2,1,0:T(8,128)(2,1)} %bitcast.51) | data formatting | bytes 54525952 | tf_op jit(solution)/shard_map/reshape | solution.py:17
  134.9 35.4 %copy.7 = bf16[32,26,128,128]{2,0,3,1:T(8,128)(2,1)} copy(bf16[32,26,128,128]{3,2,1,0:T(8,128)(2,1)} %bitcast.50) | data formatting | bytes 54525952 | tf_op jit(solution)/shard_map/reshape | solution.py:17
  170.3 0.1 reshape.75
  170.3 0.3 reduce-window.24
  170.6 0.1 slice.23
  170.7 24.7 %fusion.23 = bf16[512,3328]{0,1:T(8,128)(2,1)} fusion(bf16[512,4096]{1,0:T(8,128)(2,1)} %all-gather.2.cloned.1.call-done, bf16[416,8,32,128]{3,2,1,0:T(8,128)(2,1)} %bitcast.52), kind=kOutput, calls=%fused_computation.25 | convolution fusion | flops 13960347648 | bytes 34865152 | tf_op jit(solution)/shard_map/dot_general | solution.py:27
  195.5 24.5 %fusion.26 = bf16[512,3328]{0,1:T(8,128)(2,1)} fusion(bf16[512,4096]{1,0:T(8,128)(2,1)} %all-gather.2.cloned.1.call-done, bf16[416,8,32,128]{3,2,1,0:T(8,128)(2,1)} %bitcast.53), kind=kOutput, calls=%fused_computation.26 | convolution fusion | flops 13960347648 | bytes 34865152 | tf_op jit(solution)/shard_map/dot_general | solution.py:26
  220.0 0.1 slice_reduce_fusion
  220.1 0.1 add_bitcast_fusion
  220.2 28.0 %gather_fusion.2 = bf16[832,128,128]{2,1,0:T(8,128)(2,1)} fusion(bf16[640,128,128]{2,1,0:T(8,128)(2,1)} %param.11, s32[1024]{0:T(1024)S(1)} %pad_clamp_fusion), kind=kCustom, calls=%fused_computation.2.clone | custom fusion | bytes 54529280 | tf_op jit(solution)/shard_map/jit(_take)/gather | solution.py:14
  248.3 18.3 %select_multiply_fusion = bf16[832,128,128]{2,1,0:T(8,128)(2,1)} fusion(bf16[832,128,128]{2,1,0:T(8,128)(2,1)} %gather_fusion.2, pred[832]{0:T(1024)(128)(4,1)S(1)} %get-tuple-element.10, bf16[832]{0:T(1024)(128)(2,1)S(1)} %convert_element_type.47), kind=kLoop, calls=%fused_computation.12 | loop fusion | flops 27262976 | bytes 54528448 | tf_op jit(solution)/shard_map/mul | solution.py:14
  266.6 24.4 %copy.9 = bf16[26,32,128,128]{3,1,2,0:T(8,128)(2,1)} copy(bf16[26,32,128,128]{3,2,1,0:T(8,128)(2,1)} %bitcast.49) | data formatting | bytes 54525952 | tf_op jit(solution)/shard_map/reshape | solution.py:17
  291.0 61.4 %all-reduce.5.cloned.1.call-done = (bf16[512,3328]{0,1:T(8,128)(2,1)}, bf16[512,3328]{0,1:T(8,128)(2,1)}) async-done(((bf16[512,3328]{0,1:T(8,128)(2,1)}, bf16[512,3328]{0,1:T(8,128)(2,1)}), (bf16[512,3328]{0,1:T(8,128)(2,1)}, bf16[512,3328]{0,1:T(8,128)(2,1)})) %all-reduce.5.cloned.1.call-update) | async-done | bytes 6815760 | tf_op jit(solution)/shard_map/psum | solution.py:30
  352.4 26.2 %fusion.20 = bf16[512,4096]{1,0:T(8,128)(2,1)} fusion(bf16[416,8,32,128]{3,2,1,0:T(8,128)(2,1)} %bitcast.54, bf16[512,3328]{0,1:T(8,128)(2,1)} %get-tuple-element.6, bf16[512,3328]{0,1:T(8,128)(2,1)} %get-tuple-element.7), kind=kOutput, calls=%fused_computation.24 | convolution fusion | flops 13974372352 | bytes 38273024 | tf_op jit(solution)/shard_map/dot_general | solution.py:33
  378.6 88.9 %reduce-scatter.2.cloned.1.call-done = bf16[64,4096]{1,0:T(8,128)(2,1)} async-done(((bf16[512,4096]{1,0:T(8,128)(2,1)}), bf16[64,4096]{1,0:T(8,128)(2,1)}) %reduce-scatter.2.cloned.1.call-update) | async-done | bytes 524304 | tf_op jit(solution)/shard_map/reduce_scatter | solution.py:34
  (18 shorter events, 0.2 us)
Async XLA Ops:
  6.5 164.2 %all-gather.2.cloned.1.call-start = ((), (), s32[]{:S(2)}) async-start(), calls=%async_computation.1 | async-start | bytes 4718592 | tf_op jit(solution)/shard_map/all_gather | solution.py:25
  7.3 345.1 %all-reduce.5.cloned.1.call-start = ((), (), s32[]{:S(2)}) async-start(), calls=%async_computation.3 | async-start | bytes 13631488 | tf_op jit(solution)/shard_map/psum | solution.py:30
  134.9 35.4 %copy-start = (s32[26,32]{1,0:T(8,128)S(1)}, s32[26,32]{1,0:T(8,128)}, u32[]{:S(2)}) copy-start(s32[26,32]{1,0:T(8,128)} %param.13) | copy-start | bytes 9988
  220.0 247.5 %reduce-scatter.2.cloned.1.call-start = ((), (), s32[]{:S(2)}) async-start(), calls=%async_computation.2 | async-start | bytes 4718592 | tf_op jit(solution)/shard_map/reduce_scatter | solution.py:34
Sparse Core Ops, SparseCore 0:
  9.5 76.0 all-gather.1
  220.1 132.2 all-reduce.4
  378.7 88.7 reduce-scatter.1
where the time goes:
time: 482 us; the launch traced here: 474 us
  local copies, waits for them, and re-layouts  178 us (37%)
  waiting for transfers between devices  151 us (31%)
  matrix products  75.4 us (16%)
  other arithmetic  56.1 us (12%)
  between operations  13.4 us (3%)
    reshape x3, local copies, waits for them, and re-layouts, dense_tile(): picked.reshape(in_blocks, out_blocks, block, block).transpose(0, 2, 1, 3)  94.8 us
    reduce_scatter x1, waiting for transfers between devices, local(): lax.psum_scatter(partial_out.astype(jnp.bfloat16), 'col', scatter_dimensi...  88.9 us
    gather x3, local copies, waits for them, and re-layouts, dense_tile(): jnp.take(packed_tile, slot_index, axis=0)  82.2 us
    psum x1, waiting for transfers between devices, local(): lax.psum(up_rows.astype(jnp.bfloat16), 'row').astype(jnp.float32)  61.4 us
    mul x2, other arithmetic, dense_tile(): jnp.take(packed_tile, slot_index, axis=0)  55.2 us
    dot_general x1, matrix products, local(): jnp.dot(every_hidden, down_dense, preferred_element_type=jnp.float32)  26.2 us
    dot_general x1, matrix products, local(): up_rows = jnp.dot(segment, up_dense, preferred_element_type=jnp.float32)  24.7 us
    dot_general x1, matrix products, local(): gate_rows = jnp.dot(segment, gate_dense, preferred_element_type=jnp.float32)  24.5 us
  transfers between devices with their start and end apart: 3, of which 2 were waited for; matrix products, arithmetic and copies ran while one was open for 49% of the time, Pallas kernels for 0%

commit v1 on v0

--- a/solution.py
+++ b/solution.py
@@ -27,7 +27,7 @@
     up_rows = jnp.dot(segment, up_dense, preferred_element_type=jnp.float32)
     gate_sum, up_sum = (
         lax.psum(gate_rows.astype(jnp.bfloat16), "row").astype(jnp.float32),
-        lax.psum(up_rows.astype(jnp.bfloat16), "row").astype(jnp.float32),
+        jnp.sum(lax.all_gather(up_rows.astype(jnp.bfloat16), "row"), axis=0).astype(jnp.float32),
     )
     every_hidden = (jax.nn.silu(gate_sum) * up_sum).astype(jnp.bfloat16)
     partial_out = jnp.dot(every_hidden, down_dense, preferred_element_type=jnp.float32)

time: 482 us -> 470 us (0.975)
  waiting for transfers between devices: 151 us -> 92.9 us
  local copies, waits for them, and re-layouts: 178 us -> 203 us
  other arithmetic: 56.1 us -> 78.9 us
    psum x1, waiting for transfers between devices: 61.4 us -> 0.02 us  [local(): lax.psum(gate_rows.astype(jnp.bfloat16), 'row').astype(jnp.float32)]
    all_gather x0 -> x1, local copies, waits for them, and re-layouts: none -> 23.1 us  [local(): lax.all_gather(up_rows.astype(jnp.bfloat16), 'row')]
    reduce_sum x0 -> x1, other arithmetic: none -> 21.4 us  [local(): jnp.sum(lax.all_gather(up_rows.astype(jnp.bfloat16), 'row'), axis=0)]
  transfers between devices with their start and end apart: 3 -> 4, of which waited for: 2 -> 1; matrix products, arithmetic and copies ran while one was open for 49% -> 66% of each run, Pallas kernels for 0% -> 0%
where the time goes in v1:
time: 470 us; the launch traced here: 462 us
  local copies, waits for them, and re-layouts  203 us (43%)
  waiting for transfers between devices  92.9 us (20%)
  other arithmetic  78.9 us (17%)
  matrix products  74.1 us (16%)
  between operations  13.4 us (3%)
    reshape x3, local copies, waits for them, and re-layouts, dense_tile(): picked.reshape(in_blocks, out_blocks, block, block).transpose(0, 2, 1, 3)  96.1 us
    reduce_scatter x1, waiting for transfers between devices, local(): lax.psum_scatter(partial_out.astype(jnp.bfloat16), 'col', scatter_dimensi...  92.1 us
    gather x3, local copies, waits for them, and re-layouts, dense_tile(): jnp.take(packed_tile, slot_index, axis=0)  82 us
    mul x2, other arithmetic, dense_tile(): jnp.take(packed_tile, slot_index, axis=0)  56.6 us
    dot_general x1, matrix products, local(): jnp.dot(every_hidden, down_dense, preferred_element_type=jnp.float32)  25.1 us
    dot_general x1, matrix products, local(): up_rows = jnp.dot(segment, up_dense, preferred_element_type=jnp.float32)  24.7 us
    dot_general x1, matrix products, local(): gate_rows = jnp.dot(segment, gate_dense, preferred_element_type=jnp.float32)  24.3 us
    all_gather x1, local copies, waits for them, and re-layouts, local(): lax.all_gather(up_rows.astype(jnp.bfloat16), 'row')  23.1 us
  transfers between devices with their start and end apart: 4, of which 1 were waited for; matrix products, arithmetic and copies ran while one was open for 66% of the time, Pallas kernels for 0%

profile of v1, /device:TPU:0, one launch (start us, length us, event | category | flops | bytes accessed | tf_op | source)
XLA Modules:
  0.0 462.0 jit_solution(12038373193838142047)
XLA Ops:
  6.5 0.7 all-gather.4.cloned.1.call-update
  7.3 0.8 reshape.68
  8.1 0.3 reduce-window.16
  8.4 0.1 slice.20
  8.5 0.1 slice_reduce_fusion.1
  8.6 0.1 add_bitcast_fusion.1
  8.7 27.2 %gather_fusion = bf16[832,128,128]{2,1,0:T(8,128)(2,1)} fusion(bf16[640,128,128]{2,1,0:T(8,128)(2,1)} %param.9, s32[1024]{0:T(1024)S(1)} %pad_clamp_fusion.1), kind=kCustom, calls=%fused_computation.clone | custom fusion | bytes 54529280 | tf_op jit(solution)/shard_map/jit(_take)/gather | solution.py:14
  35.9 27.1 %gather_fusion.1 = bf16[832,128,128]{2,1,0:T(8,128)(2,1)} fusion(bf16[640,128,128]{2,1,0:T(8,128)(2,1)} %param.10, s32[1024]{0:T(1024)S(1)} %pad_clamp_fusion.1), kind=kCustom, calls=%fused_computation.1.clone | custom fusion | bytes 54529280 | tf_op jit(solution)/shard_map/jit(_take)/gather | solution.py:14
  62.9 36.9 %select_multiply_fusion.2 = (bf16[832,128,128]{2,1,0:T(8,128)(2,1)}, bf16[832,128,128]{2,1,0:T(8,128)(2,1)}) fusion(bf16[832,128,128]{2,1,0:T(8,128)(2,1)} %gather_fusion, pred[832]{0:T(1024)(128)(4,1)S(1)} %get-tuple-element.6, bf16[832]{0:T(1024)(128)(2,1)S(1)} %convert_element_type.41, bf16[832,128,128]{2,1,0:T(8,128)(2,1)} %gather_fusion.1), kind=kLoop, calls=%fused_computation.14 | loop fusion | flops 54525952 | bytes 109054400 | tf_op jit(solution)/shard_map/mul | solution.py:14
  99.9 35.4 %copy.8 = bf16[32,26,128,128]{2,0,3,1:T(8,128)(2,1)} copy(bf16[32,26,128,128]{3,2,1,0:T(8,128)(2,1)} %bitcast.53) | data formatting | bytes 54525952 | tf_op jit(solution)/shard_map/reshape | solution.py:17
  135.2 24.7 %fusion.23 = bf16[512,3328]{0,1:T(8,128)(2,1)} fusion(bf16[512,4096]{1,0:T(8,128)(2,1)} %all-gather.4.cloned.1.call-done, bf16[416,8,32,128]{3,2,1,0:T(8,128)(2,1)} %bitcast.56), kind=kOutput, calls=%fused_computation.25 | convolution fusion | flops 13960347648 | bytes 34865152 | tf_op jit(solution)/shard_map/dot_general | solution.py:27
  160.1 36.3 %copy.7 = bf16[32,26,128,128]{2,0,3,1:T(8,128)(2,1)} copy(bf16[32,26,128,128]{3,2,1,0:T(8,128)(2,1)} %bitcast.52) | data formatting | bytes 54525952 | tf_op jit(solution)/shard_map/reshape | solution.py:17
  196.5 0.3 reduce-window.24
  196.7 0.1 slice.23
  196.8 0.1 slice_reduce_fusion
  197.0 0.1 add_bitcast_fusion
  197.1 27.8 %gather_fusion.2 = bf16[832,128,128]{2,1,0:T(8,128)(2,1)} fusion(bf16[640,128,128]{2,1,0:T(8,128)(2,1)} %param.11, s32[1024]{0:T(1024)S(1)} %pad_clamp_fusion), kind=kCustom, calls=%fused_computation.2.clone | custom fusion | bytes 54529280 | tf_op jit(solution)/shard_map/jit(_take)/gather | solution.py:14
  224.9 24.3 %fusion.26 = bf16[512,3328]{0,1:T(8,128)(2,1)} fusion(bf16[512,4096]{1,0:T(8,128)(2,1)} %all-gather.4.cloned.1.call-done, bf16[416,8,32,128]{3,2,1,0:T(8,128)(2,1)} %bitcast.54), kind=kOutput, calls=%fused_computation.26 | convolution fusion | flops 13960347648 | bytes 34865152 | tf_op jit(solution)/shard_map/dot_general | solution.py:26
  249.2 19.7 %select_multiply_fusion = bf16[832,128,128]{2,1,0:T(8,128)(2,1)} fusion(bf16[832,128,128]{2,1,0:T(8,128)(2,1)} %gather_fusion.2, pred[832]{0:T(1024)(128)(4,1)S(1)} %get-tuple-element.8, bf16[832]{0:T(1024)(128)(2,1)S(1)} %convert_element_type.49), kind=kLoop, calls=%fused_computation.12 | loop fusion | flops 27262976 | bytes 54528448 | tf_op jit(solution)/shard_map/mul | solution.py:14
  268.9 24.4 %copy.9 = bf16[26,32,128,128]{3,1,2,0:T(8,128)(2,1)} copy(bf16[26,32,128,128]{3,2,1,0:T(8,128)(2,1)} %bitcast.51) | data formatting | bytes 54525952 | tf_op jit(solution)/shard_map/reshape | solution.py:17
  293.4 23.1 %reshape.104 = bf16[4,512,3328]{1,0,2:T(4,128)(2,1)} reshape(bf16[2048,3328]{0,1:T(8,128)(2,1)} %all-gather.6.cloned.1.call-done) | data formatting | bytes 27262976 | tf_op jit(solution)/shard_map/all_gather | solution.py:30
  316.5 21.4 %reduce_sum.12 = bf16[512,3328]{0,1:T(8,128)(2,1)S(1)} reduce(bf16[4,512,3328]{1,0,2:T(4,128)(2,1)} %reshape.104, bf16[]{:T(256)} %constant.27.clone.1), dimensions={0}, to_apply=%region_3.5 | reduce | flops 5111808 | bytes 17039362 | tf_op jit(solution)/shard_map/reduce_sum | solution.py:30
  337.9 25.1 %fusion.20 = bf16[512,4096]{1,0:T(8,128)(2,1)} fusion(bf16[416,8,32,128]{3,2,1,0:T(8,128)(2,1)} %bitcast.55, bf16[512,3328]{0,1:T(8,128)(2,1)S(1)} %reduce_sum.12, bf16[512,3328]{0,1:T(8,128)(2,1)} %all-reduce.4.cloned.1.call-done), kind=kOutput, calls=%fused_computation.24 | convolution fusion | flops 13974372352 | bytes 38273024 | tf_op jit(solution)/shard_map/dot_general | solution.py:33
  363.1 92.1 %reduce-scatter.2.cloned.1.call-done = bf16[64,4096]{1,0:T(8,128)(2,1)} async-done(((bf16[512,4096]{1,0:T(8,128)(2,1)}), bf16[64,4096]{1,0:T(8,128)(2,1)}) %reduce-scatter.2.cloned.1.call-update) | async-done | bytes 524304 | tf_op jit(solution)/shard_map/reduce_scatter | solution.py:34
  (23 shorter events, 0.4 us)
Async XLA Ops:
  6.5 128.7 %all-gather.4.cloned.1.call-start = ((), (), s32[]{:S(2)}) async-start(), calls=%async_computation.1 | async-start | bytes 4718592 | tf_op jit(solution)/shard_map/all_gather | solution.py:25
  7.3 286.1 %all-gather.6.cloned.1.call-start = ((), (), s32[]{:S(2)}) async-start(), calls=%async_computation.4 | async-start | bytes 17039360 | tf_op jit(solution)/shard_map/all_gather | solution.py:30
  160.0 177.9 %all-reduce.4.cloned.1.call-start = ((), (), s32[]{:S(2)}) async-start(), calls=%async_computation.2 | async-start | bytes 6815744 | tf_op jit(solution)/shard_map/psum | solution.py:29
  160.0 36.3 %copy-start = (s32[26,32]{1,0:T(8,128)S(1)}, s32[26,32]{1,0:T(8,128)}, u32[]{:S(2)}) copy-start(s32[26,32]{1,0:T(8,128)} %param.13) | copy-start | bytes 9988
  249.2 206.1 %reduce-scatter.2.cloned.1.call-start = ((), (), s32[]{:S(2)}) async-start(), calls=%async_computation.3 | async-start | bytes 4718592 | tf_op jit(solution)/shard_map/reduce_scatter | solution.py:34
Sparse Core Ops, SparseCore 0:
  9.5 76.0 all-gather.3
  160.1 91.6 all-gather.5
  254.2 72.6 all-reduce.3
  363.2 91.9 reduce-scatter.1
